TPU v7x, 512 devices: a whole 4x8x8 slice. The times are simulated.
512 devices in a mesh: area: 128 (over z, y, core), blk: 4 (over x).
Axes of the slice: x: 4, y: 8, z: 8, core: 2. Of those that a mesh axis runs over, the one named last changes fastest.
Arguments:
- activity: float32 [1024, 4, 64, 128], P('area', 'blk'), may hold values from -8 to 8
- ext_input: bfloat16 [1024, 4, 64, 128], P('area', 'blk'), may hold values from -5 to 5
- weights: bfloat16 [384, 4, 128, 512], P('area', 'blk'), may hold values from -0.25 to 0.25
- slot_dst: int32 [384], P('area'), may hold values from 0 to 7
- slot_src: int32 [384], P('area'), may hold values from 0 to 1023, as said below
- slot_count: int32 [128], P('area'), may hold values from 3 to 3, as said below
- hebb_mask: int32 [384], P('area'), may hold values 0 or 1
Outputs:
- final_activity: float32 [1024, 4, 64, 128], P('area', 'blk')
- plasticity: bfloat16 [384, 4, 128, 512], P('area', 'blk')
Inputs may be any that keep to these rules, and one draw needn't show every extreme that they name: Index i of area holds area i // 4; sources lie in areas listed for it by a connectome over the areas that always lists the area itself, the areas beside it on both sides (counted round) and the opposite one. Slots 0, 1 and 2 of index i of area have their source sub-blocks held by indices (i - 1) mod 128, (i + 1) mod 128 and (i + 64) mod 128. Among the occupied slots of one index of area, at most 1 have source sub-blocks held by one index of area (slot_src // 8); some index of area reaches 1. `slot_count`: some index of area has all 3 slots occupied.
All inputs are finite; a program needn't handle non-finite values. No bound on the sum of `hebb_mask` on one device may be relied on, other than what follows from the above.
Results may differ from a plain program's by a relative error of at most 0.014.
Values may be sent and summed in bfloat16 or wider, within the bound.
No kernel may reach another device: no remote copies, remote signals or barrier semaphores. Data moves between devices by JAX's collectives and lax.ppermute only.
A program may use at most 64 MiB of HBM per device.

v0:
```python
import jax
import jax.numpy as jnp
from jax import lax
from jax.sharding import PartitionSpec as P

STEPS = 4
euler_step = 0.5


def centre(x):
    xf = x.astype(jnp.float32)
    return (xf - jnp.mean(xf, axis=-2, keepdims=True)).astype(jnp.bfloat16)


def body(activity, ext_input, weights, slot_dst, slot_src, slot_count, hebb_mask):
    n_areas = lax.axis_size("area")
    n_blk = lax.axis_size("blk")
    my_blk = lax.axis_index("blk")
    sub_dev = activity.shape[0]
    trials = activity.shape[2]
    quarter = activity.shape[3]
    slot_cap = slot_src.shape[0]
    sub_width = weights.shape[3]
    offsets = (-1, 1, n_areas // 2)
    occupied = jnp.arange(slot_cap) < slot_count[0]
    select = ((slot_dst[:, None] == jnp.arange(sub_dev)[None, :]) & occupied[:, None]).astype(
        jnp.float32
    )
    wanted = jnp.clip(slot_src % sub_dev, 0, sub_dev - 1).astype(jnp.int32)
    provide = []
    for k in range(slot_cap):
        perm = [(i, (i + offsets[k]) % n_areas) for i in range(n_areas)]
        provide.append(lax.ppermute(wanted[k], "area", perm))
    w_split = weights[:, 0].reshape(slot_cap, quarter, n_blk, quarter)
    w_parts = lax.all_to_all(w_split, "blk", split_axis=2, concat_axis=2, tiled=True)
    part_of_shift = (my_blk - jnp.arange(n_blk)) % n_blk
    w_shift = jnp.take(w_parts, part_of_shift, axis=2).transpose(0, 2, 1, 3)

    def n_of(area_idx, blk_idx):
        return area_idx * n_blk + blk_idx

    def exchange(rate_own):
        got = []
        for k in range(slot_cap):
            payload = lax.dynamic_index_in_dim(rate_own, provide[k], 0, keepdims=False)
            per_shift = []
            for s in range(n_blk):
                perm = [
                    (n_of(i, b), n_of((i - offsets[k]) % n_areas, (b + s) % n_blk))
                    for i in range(n_areas)
                    for b in range(n_blk)
                ]
                per_shift.append(lax.ppermute(payload, ("area", "blk"), perm))
            got.append(jnp.stack(per_shift))
        return jnp.stack(got)

    current = activity[:, 0]
    drive_in = ext_input[:, 0].astype(jnp.float32)
    rate_own = jnp.tanh(current).astype(jnp.bfloat16)
    pre_list = []
    post_list = []
    for step_idx in range(STEPS):
        presyn = exchange(rate_own)
        contrib = jnp.einsum("ksnq,ksqv->ksnv", presyn, w_shift, preferred_element_type=jnp.float32)
        partial_value = jnp.einsum(
            "kd,ksnv->sdnv", select, contrib, precision=lax.Precision.HIGHEST
        )
        summed = jnp.sum(partial_value.astype(jnp.bfloat16).astype(jnp.float32), axis=0)
        current = current + euler_step * (summed - current + drive_in)
        rate_own = jnp.tanh(current).astype(jnp.bfloat16)
        pre_list.append(presyn[:, 0])
        post_list.append(rate_own)
    final_state = current[:, None]
    pre_centered = centre(jnp.stack(pre_list, axis=1))
    post_centered = centre(jnp.stack(post_list, axis=0))
    post_sel = jnp.take(post_centered, slot_dst, axis=1).transpose(1, 0, 2, 3)
    post_whole = lax.all_gather(post_sel, "blk", axis=3, tiled=True)
    change = jnp.einsum(
        "ktnq,ktnu->kqu", pre_centered, post_whole, preferred_element_type=jnp.float32
    )
    gate_on = (occupied & (hebb_mask == 1)).astype(jnp.float32)
    norm_scale = (STEPS * trials) ** (-0.5)
    plasticity = (change * gate_on[:, None, None] * norm_scale).astype(jnp.bfloat16)[:, None]
    return (final_state, plasticity)


def solution(mesh):
    in_specs = (
        P("area", "blk", None, None),
        P("area", "blk", None, None),
        P("area", "blk", None, None),
        P("area"),
        P("area"),
        P("area"),
        P("area"),
    )
    out_specs = (P("area", "blk", None, None), P("area", "blk", None, None))
    return jax.shard_map(body, mesh=mesh, in_specs=in_specs, out_specs=out_specs, check_vma=False)
```

profile of v0, /device:TPU:2, one launch (start us, length us, event | category | flops | bytes accessed | tf_op | source)
XLA Modules:
  0.0 270.8 jit_solution(7294866537927108117)
XLA Ops:
  2.0 13.3 %collective-permute-start = (s32[]{:T(128)}, s32[]{:T(128)}, u32[]{:S(2)}, u32[]{:S(2)}) collective-permute-start(s32[]{:T(128)} %bitcast.2), channel_id=1, source_target_pairs={{0,508},{4,0},{8,4},{12,8},{16,12},{20,16},{24,20},{28,24},{32,28}... | collective-permute-start | bytes 20 | tf_op jit(solution)/shard_map/ppermute | solution.py:33
  21.3 5.0 %all-to-all-start = ((bf16[3,128,4,128]{3,1,0,2:T(8,128)(2,1)}), bf16[3,128,4,128]{3,1,0,2:T(8,128)(2,1)S(1)}, u32[]{:S(2)}, u32[]{:S(2)}) async-start(bf16[3,128,4,128]{3,1,0,2:T(8,128)(2,1)} %copy.71), calls=%async_computation | async-start | bytes 786432 | tf_op jit(solution)/shard_map/all_to_all | solution.py:35
  38.5 4.2 %collective-permute-start.2 = (bf16[64,128]{1,0:T(8,128)(2,1)S(1)}, bf16[64,128]{1,0:T(8,128)(2,1)S(1)}, u32[]{:S(2)}, u32[]{:S(2)}) collective-permute-start(bf16[64,128]{1,0:T(8,128)(2,1)S(1)} %get-tuple-element.28), channel_id=1, source_target_pairs={{0,5},{1,6},{2,7},{3,4},{4,9},{5,10},{6,11},{7,8},{8,13},{9,14},{1... | collective-permute-start | bytes 49160 | tf_op jit(solution)/shard_map/ppermute | solution.py:53
  48.2 7.0 %collective-permute-start.13 = (bf16[64,128]{1,0:T(8,128)(2,1)S(1)}, bf16[64,128]{1,0:T(8,128)(2,1)S(1)}, u32[]{:S(2)}, u32[]{:S(2)}) collective-permute-start(bf16[64,128]{1,0:T(8,128)(2,1)S(1)} %get-tuple-element.29), channel_id=1, source_target_pairs={{0,258},{1,259},{2,256},{3,257},{4,262},{5,263},{6,260},{7,261},{8... | collective-permute-start | bytes 49160 | tf_op jit(solution)/shard_map/ppermute | solution.py:53
  55.2 6.4 %collective-permute-start.12 = (bf16[64,128]{1,0:T(8,128)(2,1)S(1)}, bf16[64,128]{1,0:T(8,128)(2,1)S(1)}, u32[]{:S(2)}, u32[]{:S(2)}) collective-permute-start(bf16[64,128]{1,0:T(8,128)(2,1)S(1)} %get-tuple-element.29), channel_id=1, source_target_pairs={{0,257},{1,258},{2,259},{3,256},{4,261},{5,262},{6,263},{7,260},{8... | collective-permute-start | bytes 49160 | tf_op jit(solution)/shard_map/ppermute | solution.py:53
  61.6 5.7 %collective-permute-start.11 = (bf16[64,128]{1,0:T(8,128)(2,1)S(1)}, bf16[64,128]{1,0:T(8,128)(2,1)S(1)}, u32[]{:S(2)}, u32[]{:S(2)}) collective-permute-start(bf16[64,128]{1,0:T(8,128)(2,1)S(1)} %get-tuple-element.29), channel_id=1, source_target_pairs={{0,256},{1,257},{2,258},{3,259},{4,260},{5,261},{6,262},{7,263},{8... | collective-permute-start | bytes 49160 | tf_op jit(solution)/shard_map/ppermute | solution.py:53
  71.1 5.5 %collective-permute-start.8 = (bf16[64,128]{1,0:T(8,128)(2,1)S(1)}, bf16[64,128]{1,0:T(8,128)(2,1)S(1)}, u32[]{:S(2)}, u32[]{:S(2)}) collective-permute-start(bf16[64,128]{1,0:T(8,128)(2,1)S(1)} %get-tuple-element.30), channel_id=1, source_target_pairs={{0,510},{1,511},{2,508},{3,509},{4,2},{5,3},{6,0},{7,1},{8,6},{9,7... | collective-permute-start | bytes 49160 | tf_op jit(solution)/shard_map/ppermute | solution.py:53
  76.6 4.9 %collective-permute-start.7 = (bf16[64,128]{1,0:T(8,128)(2,1)S(1)}, bf16[64,128]{1,0:T(8,128)(2,1)S(1)}, u32[]{:S(2)}, u32[]{:S(2)}) collective-permute-start(bf16[64,128]{1,0:T(8,128)(2,1)S(1)} %get-tuple-element.30), channel_id=1, source_target_pairs={{0,509},{1,510},{2,511},{3,508},{4,1},{5,2},{6,3},{7,0},{8,5},{9,6... | collective-permute-start | bytes 49160 | tf_op jit(solution)/shard_map/ppermute | solution.py:53
  97.5 8.4 %collective-permute-start.26 = (bf16[64,128]{1,0:T(8,128)(2,1)S(1)}, bf16[64,128]{1,0:T(8,128)(2,1)S(1)}, u32[]{:S(2)}, u32[]{:S(2)}) collective-permute-start(bf16[64,128]{1,0:T(8,128)(2,1)S(1)} %get-tuple-element.26), channel_id=1, source_target_pairs={{0,259},{1,256},{2,257},{3,258},{4,263},{5,260},{6,261},{7,262},{8... | collective-permute-start | bytes 49160 | tf_op jit(solution)/shard_map/ppermute | solution.py:53
  109.4 9.0 %collective-permute-start.24 = (bf16[64,128]{1,0:T(8,128)(2,1)S(1)}, bf16[64,128]{1,0:T(8,128)(2,1)S(1)}, u32[]{:S(2)}, u32[]{:S(2)}) collective-permute-start(bf16[64,128]{1,0:T(8,128)(2,1)S(1)} %get-tuple-element.26), channel_id=1, source_target_pairs={{0,257},{1,258},{2,259},{3,256},{4,261},{5,262},{6,263},{7,260},{8... | collective-permute-start | bytes 49160 | tf_op jit(solution)/shard_map/ppermute | solution.py:53
  120.4 6.4 %collective-permute-start.22 = (bf16[64,128]{1,0:T(8,128)(2,1)S(1)}, bf16[64,128]{1,0:T(8,128)(2,1)S(1)}, u32[]{:S(2)}, u32[]{:S(2)}) collective-permute-start(bf16[64,128]{1,0:T(8,128)(2,1)S(1)} %get-tuple-element.27), channel_id=1, source_target_pairs={{0,511},{1,508},{2,509},{3,510},{4,3},{5,0},{6,1},{7,2},{8,7},{9,4... | collective-permute-start | bytes 49160 | tf_op jit(solution)/shard_map/ppermute | solution.py:53
  126.8 4.5 %collective-permute-start.21 = (bf16[64,128]{1,0:T(8,128)(2,1)S(1)}, bf16[64,128]{1,0:T(8,128)(2,1)S(1)}, u32[]{:S(2)}, u32[]{:S(2)}) collective-permute-start(bf16[64,128]{1,0:T(8,128)(2,1)S(1)} %get-tuple-element.27), channel_id=1, source_target_pairs={{0,510},{1,511},{2,508},{3,509},{4,2},{5,3},{6,0},{7,1},{8,6},{9,7... | collective-permute-start | bytes 49160 | tf_op jit(solution)/shard_map/ppermute | solution.py:53
  131.3 4.9 %collective-permute-start.20 = (bf16[64,128]{1,0:T(8,128)(2,1)S(1)}, bf16[64,128]{1,0:T(8,128)(2,1)S(1)}, u32[]{:S(2)}, u32[]{:S(2)}) collective-permute-start(bf16[64,128]{1,0:T(8,128)(2,1)S(1)} %get-tuple-element.27), channel_id=1, source_target_pairs={{0,509},{1,510},{2,511},{3,508},{4,1},{5,2},{6,3},{7,0},{8,5},{9,6... | collective-permute-start | bytes 49160 | tf_op jit(solution)/shard_map/ppermute | solution.py:53
  151.3 9.2 %collective-permute-start.38 = (bf16[64,128]{1,0:T(8,128)(2,1)S(1)}, bf16[64,128]{1,0:T(8,128)(2,1)S(1)}, u32[]{:S(2)}, u32[]{:S(2)}) collective-permute-start(bf16[64,128]{1,0:T(8,128)(2,1)S(1)} %get-tuple-element.23), channel_id=1, source_target_pairs={{0,259},{1,256},{2,257},{3,258},{4,263},{5,260},{6,261},{7,262},{8... | collective-permute-start | bytes 49160 | tf_op jit(solution)/shard_map/ppermute | solution.py:53
  163.5 8.5 %collective-permute-start.36 = (bf16[64,128]{1,0:T(8,128)(2,1)S(1)}, bf16[64,128]{1,0:T(8,128)(2,1)S(1)}, u32[]{:S(2)}, u32[]{:S(2)}) collective-permute-start(bf16[64,128]{1,0:T(8,128)(2,1)S(1)} %get-tuple-element.23), channel_id=1, source_target_pairs={{0,257},{1,258},{2,259},{3,256},{4,261},{5,262},{6,263},{7,260},{8... | collective-permute-start | bytes 49160 | tf_op jit(solution)/shard_map/ppermute | solution.py:53
  174.5 6.3 %collective-permute-start.34 = (bf16[64,128]{1,0:T(8,128)(2,1)S(1)}, bf16[64,128]{1,0:T(8,128)(2,1)S(1)}, u32[]{:S(2)}, u32[]{:S(2)}) collective-permute-start(bf16[64,128]{1,0:T(8,128)(2,1)S(1)} %get-tuple-element.24), channel_id=1, source_target_pairs={{0,511},{1,508},{2,509},{3,510},{4,3},{5,0},{6,1},{7,2},{8,7},{9,4... | collective-permute-start | bytes 49160 | tf_op jit(solution)/shard_map/ppermute | solution.py:53
  180.8 5.1 %collective-permute-start.33 = (bf16[64,128]{1,0:T(8,128)(2,1)S(1)}, bf16[64,128]{1,0:T(8,128)(2,1)S(1)}, u32[]{:S(2)}, u32[]{:S(2)}) collective-permute-start(bf16[64,128]{1,0:T(8,128)(2,1)S(1)} %get-tuple-element.24), channel_id=1, source_target_pairs={{0,510},{1,511},{2,508},{3,509},{4,2},{5,3},{6,0},{7,1},{8,6},{9,7... | collective-permute-start | bytes 49160 | tf_op jit(solution)/shard_map/ppermute | solution.py:53
  185.9 4.8 %collective-permute-start.32 = (bf16[64,128]{1,0:T(8,128)(2,1)S(1)}, bf16[64,128]{1,0:T(8,128)(2,1)S(1)}, u32[]{:S(2)}, u32[]{:S(2)}) collective-permute-start(bf16[64,128]{1,0:T(8,128)(2,1)S(1)} %get-tuple-element.24), channel_id=1, source_target_pairs={{0,509},{1,510},{2,511},{3,508},{4,1},{5,2},{6,3},{7,0},{8,5},{9,6... | collective-permute-start | bytes 49160 | tf_op jit(solution)/shard_map/ppermute | solution.py:53
  206.0 8.7 %collective-permute-start.50 = (bf16[64,128]{1,0:T(8,128)(2,1)S(1)}, bf16[64,128]{1,0:T(8,128)(2,1)S(1)}, u32[]{:S(2)}, u32[]{:S(2)}) collective-permute-start(bf16[64,128]{1,0:T(8,128)(2,1)S(1)} %get-tuple-element.20), channel_id=1, source_target_pairs={{0,259},{1,256},{2,257},{3,258},{4,263},{5,260},{6,261},{7,262},{8... | collective-permute-start | bytes 49160 | tf_op jit(solution)/shard_map/ppermute | solution.py:53
  218.2 9.0 %collective-permute-start.48 = (bf16[64,128]{1,0:T(8,128)(2,1)S(1)}, bf16[64,128]{1,0:T(8,128)(2,1)S(1)}, u32[]{:S(2)}, u32[]{:S(2)}) collective-permute-start(bf16[64,128]{1,0:T(8,128)(2,1)S(1)} %get-tuple-element.20), channel_id=1, source_target_pairs={{0,257},{1,258},{2,259},{3,256},{4,261},{5,262},{6,263},{7,260},{8... | collective-permute-start | bytes 49160 | tf_op jit(solution)/shard_map/ppermute | solution.py:53
  229.2 6.4 %collective-permute-start.46 = (bf16[64,128]{1,0:T(8,128)(2,1)S(1)}, bf16[64,128]{1,0:T(8,128)(2,1)S(1)}, u32[]{:S(2)}, u32[]{:S(2)}) collective-permute-start(bf16[64,128]{1,0:T(8,128)(2,1)S(1)} %get-tuple-element.21), channel_id=1, source_target_pairs={{0,511},{1,508},{2,509},{3,510},{4,3},{5,0},{6,1},{7,2},{8,7},{9,4... | collective-permute-start | bytes 49160 | tf_op jit(solution)/shard_map/ppermute | solution.py:53
  235.6 4.5 %collective-permute-start.45 = (bf16[64,128]{1,0:T(8,128)(2,1)S(1)}, bf16[64,128]{1,0:T(8,128)(2,1)S(1)}, u32[]{:S(2)}, u32[]{:S(2)}) collective-permute-start(bf16[64,128]{1,0:T(8,128)(2,1)S(1)} %get-tuple-element.21), channel_id=1, source_target_pairs={{0,510},{1,511},{2,508},{3,509},{4,2},{5,3},{6,0},{7,1},{8,6},{9,7... | collective-permute-start | bytes 49160 | tf_op jit(solution)/shard_map/ppermute | solution.py:53
  240.1 4.9 %collective-permute-start.44 = (bf16[64,128]{1,0:T(8,128)(2,1)S(1)}, bf16[64,128]{1,0:T(8,128)(2,1)S(1)}, u32[]{:S(2)}, u32[]{:S(2)}) collective-permute-start(bf16[64,128]{1,0:T(8,128)(2,1)S(1)} %get-tuple-element.21), channel_id=1, source_target_pairs={{0,509},{1,510},{2,511},{3,508},{4,1},{5,2},{6,3},{7,0},{8,5},{9,6... | collective-permute-start | bytes 49160 | tf_op jit(solution)/shard_map/ppermute | solution.py:53
  253.1 16.6 %all_gather.3 = bf16[3,4,64,512]{3,2,1,0:T(8,128)(2,1)S(1)} all-gather(bf16[3,4,64,128]{3,2,1,0:T(8,128)(2,1)S(1)} %broadcast_select_fusion), channel_id=1, replica_groups=mesh['area'=128,'blk'=4] {'blk'}, dimensions={3}, use_global_device_ids=true | all-gather | bytes 983040 | tf_op jit(solution)/shard_map/all_gather | solution.py:77
  (142 shorter events, 93.8 us)
Async XLA Ops:
  2.0 25.8 %collective-permute-start = (s32[]{:T(128)}, s32[]{:T(128)}, u32[]{:S(2)}, u32[]{:S(2)}) collective-permute-start(s32[]{:T(128)} %bitcast.2), channel_id=1, source_target_pairs={{0,508},{4,0},{8,4},{12,8},{16,12},{20,16},{24,20},{28,24},{32,28}... | collective-permute-start | bytes 20 | tf_op jit(solution)/shard_map/ppermute | solution.py:33
  21.3 65.1 %all-to-all-start = ((bf16[3,128,4,128]{3,1,0,2:T(8,128)(2,1)}), bf16[3,128,4,128]{3,1,0,2:T(8,128)(2,1)S(1)}, u32[]{:S(2)}, u32[]{:S(2)}) async-start(bf16[3,128,4,128]{3,1,0,2:T(8,128)(2,1)} %copy.71), calls=%async_computation | async-start | bytes 786432 | tf_op jit(solution)/shard_map/all_to_all | solution.py:35
  38.5 23.1 %collective-permute-start.2 = (bf16[64,128]{1,0:T(8,128)(2,1)S(1)}, bf16[64,128]{1,0:T(8,128)(2,1)S(1)}, u32[]{:S(2)}, u32[]{:S(2)}) collective-permute-start(bf16[64,128]{1,0:T(8,128)(2,1)S(1)} %get-tuple-element.28), channel_id=1, source_target_pairs={{0,5},{1,6},{2,7},{3,4},{4,9},{5,10},{6,11},{7,8},{8,13},{9,14},{1... | collective-permute-start | bytes 49160 | tf_op jit(solution)/shard_map/ppermute | solution.py:53
  42.7 24.5 %collective-permute-start.1 = (bf16[64,128]{1,0:T(8,128)(2,1)S(1)}, bf16[64,128]{1,0:T(8,128)(2,1)S(1)}, u32[]{:S(2)}, u32[]{:S(2)}) collective-permute-start(bf16[64,128]{1,0:T(8,128)(2,1)S(1)} %get-tuple-element.28), channel_id=1, source_target_pairs={{0,4},{1,5},{2,6},{3,7},{4,8},{5,9},{6,10},{7,11},{8,12},{9,13},{1... | collective-permute-start | bytes 49160 | tf_op jit(solution)/shard_map/ppermute | solution.py:53
  45.3 25.8 %collective-permute-start.14 = (bf16[64,128]{1,0:T(8,128)(2,1)S(1)}, bf16[64,128]{1,0:T(8,128)(2,1)S(1)}, u32[]{:S(2)}, u32[]{:S(2)}) collective-permute-start(bf16[64,128]{1,0:T(8,128)(2,1)S(1)} %get-tuple-element.29), channel_id=1, source_target_pairs={{0,259},{1,256},{2,257},{3,258},{4,263},{5,260},{6,261},{7,262},{8... | collective-permute-start | bytes 49160 | tf_op jit(solution)/shard_map/ppermute | solution.py:53
  48.2 28.4 %collective-permute-start.13 = (bf16[64,128]{1,0:T(8,128)(2,1)S(1)}, bf16[64,128]{1,0:T(8,128)(2,1)S(1)}, u32[]{:S(2)}, u32[]{:S(2)}) collective-permute-start(bf16[64,128]{1,0:T(8,128)(2,1)S(1)} %get-tuple-element.29), channel_id=1, source_target_pairs={{0,258},{1,259},{2,256},{3,257},{4,262},{5,263},{6,260},{7,261},{8... | collective-permute-start | bytes 49160 | tf_op jit(solution)/shard_map/ppermute | solution.py:53
  55.2 26.3 %collective-permute-start.12 = (bf16[64,128]{1,0:T(8,128)(2,1)S(1)}, bf16[64,128]{1,0:T(8,128)(2,1)S(1)}, u32[]{:S(2)}, u32[]{:S(2)}) collective-permute-start(bf16[64,128]{1,0:T(8,128)(2,1)S(1)} %get-tuple-element.29), channel_id=1, source_target_pairs={{0,257},{1,258},{2,259},{3,256},{4,261},{5,262},{6,263},{7,260},{8... | collective-permute-start | bytes 49160 | tf_op jit(solution)/shard_map/ppermute | solution.py:53
  61.6 23.4 %collective-permute-start.11 = (bf16[64,128]{1,0:T(8,128)(2,1)S(1)}, bf16[64,128]{1,0:T(8,128)(2,1)S(1)}, u32[]{:S(2)}, u32[]{:S(2)}) collective-permute-start(bf16[64,128]{1,0:T(8,128)(2,1)S(1)} %get-tuple-element.29), channel_id=1, source_target_pairs={{0,256},{1,257},{2,258},{3,259},{4,260},{5,261},{6,262},{7,263},{8... | collective-permute-start | bytes 49160 | tf_op jit(solution)/shard_map/ppermute | solution.py:53
  93.3 25.1 %collective-permute-start.16 = (bf16[64,128]{1,0:T(8,128)(2,1)S(1)}, bf16[64,128]{1,0:T(8,128)(2,1)S(1)}, u32[]{:S(2)}, u32[]{:S(2)}) collective-permute-start(bf16[64,128]{1,0:T(8,128)(2,1)S(1)} %get-tuple-element.25), channel_id=1, source_target_pairs={{0,5},{1,6},{2,7},{3,4},{4,9},{5,10},{6,11},{7,8},{8,13},{9,14},{1... | collective-permute-start | bytes 49160 | tf_op jit(solution)/shard_map/ppermute | solution.py:53
  95.6 24.8 %collective-permute-start.15 = (bf16[64,128]{1,0:T(8,128)(2,1)S(1)}, bf16[64,128]{1,0:T(8,128)(2,1)S(1)}, u32[]{:S(2)}, u32[]{:S(2)}) collective-permute-start(bf16[64,128]{1,0:T(8,128)(2,1)S(1)} %get-tuple-element.25), channel_id=1, source_target_pairs={{0,4},{1,5},{2,6},{3,7},{4,8},{5,9},{6,10},{7,11},{8,12},{9,13},{1... | collective-permute-start | bytes 49160 | tf_op jit(solution)/shard_map/ppermute | solution.py:53
  97.5 29.3 %collective-permute-start.26 = (bf16[64,128]{1,0:T(8,128)(2,1)S(1)}, bf16[64,128]{1,0:T(8,128)(2,1)S(1)}, u32[]{:S(2)}, u32[]{:S(2)}) collective-permute-start(bf16[64,128]{1,0:T(8,128)(2,1)S(1)} %get-tuple-element.26), channel_id=1, source_target_pairs={{0,259},{1,256},{2,257},{3,258},{4,263},{5,260},{6,261},{7,262},{8... | collective-permute-start | bytes 49160 | tf_op jit(solution)/shard_map/ppermute | solution.py:53
  105.9 25.4 %collective-permute-start.25 = (bf16[64,128]{1,0:T(8,128)(2,1)S(1)}, bf16[64,128]{1,0:T(8,128)(2,1)S(1)}, u32[]{:S(2)}, u32[]{:S(2)}) collective-permute-start(bf16[64,128]{1,0:T(8,128)(2,1)S(1)} %get-tuple-element.26), channel_id=1, source_target_pairs={{0,258},{1,259},{2,256},{3,257},{4,262},{5,263},{6,260},{7,261},{8... | collective-permute-start | bytes 49160 | tf_op jit(solution)/shard_map/ppermute | solution.py:53
  109.4 26.9 %collective-permute-start.24 = (bf16[64,128]{1,0:T(8,128)(2,1)S(1)}, bf16[64,128]{1,0:T(8,128)(2,1)S(1)}, u32[]{:S(2)}, u32[]{:S(2)}) collective-permute-start(bf16[64,128]{1,0:T(8,128)(2,1)S(1)} %get-tuple-element.26), channel_id=1, source_target_pairs={{0,257},{1,258},{2,259},{3,256},{4,261},{5,262},{6,263},{7,260},{8... | collective-permute-start | bytes 49160 | tf_op jit(solution)/shard_map/ppermute | solution.py:53
  147.4 24.6 %collective-permute-start.28 = (bf16[64,128]{1,0:T(8,128)(2,1)S(1)}, bf16[64,128]{1,0:T(8,128)(2,1)S(1)}, u32[]{:S(2)}, u32[]{:S(2)}) collective-permute-start(bf16[64,128]{1,0:T(8,128)(2,1)S(1)} %get-tuple-element.22), channel_id=1, source_target_pairs={{0,5},{1,6},{2,7},{3,4},{4,9},{5,10},{6,11},{7,8},{8,13},{9,14},{1... | collective-permute-start | bytes 49160 | tf_op jit(solution)/shard_map/ppermute | solution.py:53
  149.3 25.1 %collective-permute-start.27 = (bf16[64,128]{1,0:T(8,128)(2,1)S(1)}, bf16[64,128]{1,0:T(8,128)(2,1)S(1)}, u32[]{:S(2)}, u32[]{:S(2)}) collective-permute-start(bf16[64,128]{1,0:T(8,128)(2,1)S(1)} %get-tuple-element.22), channel_id=1, source_target_pairs={{0,4},{1,5},{2,6},{3,7},{4,8},{5,9},{6,10},{7,11},{8,12},{9,13},{1... | collective-permute-start | bytes 49160 | tf_op jit(solution)/shard_map/ppermute | solution.py:53
  151.3 29.5 %collective-permute-start.38 = (bf16[64,128]{1,0:T(8,128)(2,1)S(1)}, bf16[64,128]{1,0:T(8,128)(2,1)S(1)}, u32[]{:S(2)}, u32[]{:S(2)}) collective-permute-start(bf16[64,128]{1,0:T(8,128)(2,1)S(1)} %get-tuple-element.23), channel_id=1, source_target_pairs={{0,259},{1,256},{2,257},{3,258},{4,263},{5,260},{6,261},{7,262},{8... | collective-permute-start | bytes 49160 | tf_op jit(solution)/shard_map/ppermute | solution.py:53
  160.5 25.4 %collective-permute-start.37 = (bf16[64,128]{1,0:T(8,128)(2,1)S(1)}, bf16[64,128]{1,0:T(8,128)(2,1)S(1)}, u32[]{:S(2)}, u32[]{:S(2)}) collective-permute-start(bf16[64,128]{1,0:T(8,128)(2,1)S(1)} %get-tuple-element.23), channel_id=1, source_target_pairs={{0,258},{1,259},{2,256},{3,257},{4,262},{5,263},{6,260},{7,261},{8... | collective-permute-start | bytes 49160 | tf_op jit(solution)/shard_map/ppermute | solution.py:53
  163.5 27.2 %collective-permute-start.36 = (bf16[64,128]{1,0:T(8,128)(2,1)S(1)}, bf16[64,128]{1,0:T(8,128)(2,1)S(1)}, u32[]{:S(2)}, u32[]{:S(2)}) collective-permute-start(bf16[64,128]{1,0:T(8,128)(2,1)S(1)} %get-tuple-element.23), channel_id=1, source_target_pairs={{0,257},{1,258},{2,259},{3,256},{4,261},{5,262},{6,263},{7,260},{8... | collective-permute-start | bytes 49160 | tf_op jit(solution)/shard_map/ppermute | solution.py:53
  172.0 22.3 %collective-permute-start.35 = (bf16[64,128]{1,0:T(8,128)(2,1)S(1)}, bf16[64,128]{1,0:T(8,128)(2,1)S(1)}, u32[]{:S(2)}, u32[]{:S(2)}) collective-permute-start(bf16[64,128]{1,0:T(8,128)(2,1)S(1)} %get-tuple-element.23), channel_id=1, source_target_pairs={{0,256},{1,257},{2,258},{3,259},{4,260},{5,261},{6,262},{7,263},{8... | collective-permute-start | bytes 49160 | tf_op jit(solution)/shard_map/ppermute | solution.py:53
  201.9 25.3 %collective-permute-start.40 = (bf16[64,128]{1,0:T(8,128)(2,1)S(1)}, bf16[64,128]{1,0:T(8,128)(2,1)S(1)}, u32[]{:S(2)}, u32[]{:S(2)}) collective-permute-start(bf16[64,128]{1,0:T(8,128)(2,1)S(1)} %get-tuple-element.19), channel_id=1, source_target_pairs={{0,5},{1,6},{2,7},{3,4},{4,9},{5,10},{6,11},{7,8},{8,13},{9,14},{1... | collective-permute-start | bytes 49160 | tf_op jit(solution)/shard_map/ppermute | solution.py:53
  203.9 25.3 %collective-permute-start.39 = (bf16[64,128]{1,0:T(8,128)(2,1)S(1)}, bf16[64,128]{1,0:T(8,128)(2,1)S(1)}, u32[]{:S(2)}, u32[]{:S(2)}) collective-permute-start(bf16[64,128]{1,0:T(8,128)(2,1)S(1)} %get-tuple-element.19), channel_id=1, source_target_pairs={{0,4},{1,5},{2,6},{3,7},{4,8},{5,9},{6,10},{7,11},{8,12},{9,13},{1... | collective-permute-start | bytes 49160 | tf_op jit(solution)/shard_map/ppermute | solution.py:53
  206.0 29.6 %collective-permute-start.50 = (bf16[64,128]{1,0:T(8,128)(2,1)S(1)}, bf16[64,128]{1,0:T(8,128)(2,1)S(1)}, u32[]{:S(2)}, u32[]{:S(2)}) collective-permute-start(bf16[64,128]{1,0:T(8,128)(2,1)S(1)} %get-tuple-element.20), channel_id=1, source_target_pairs={{0,259},{1,256},{2,257},{3,258},{4,263},{5,260},{6,261},{7,262},{8... | collective-permute-start | bytes 49160 | tf_op jit(solution)/shard_map/ppermute | solution.py:53
  214.7 25.4 %collective-permute-start.49 = (bf16[64,128]{1,0:T(8,128)(2,1)S(1)}, bf16[64,128]{1,0:T(8,128)(2,1)S(1)}, u32[]{:S(2)}, u32[]{:S(2)}) collective-permute-start(bf16[64,128]{1,0:T(8,128)(2,1)S(1)} %get-tuple-element.20), channel_id=1, source_target_pairs={{0,258},{1,259},{2,256},{3,257},{4,262},{5,263},{6,260},{7,261},{8... | collective-permute-start | bytes 49160 | tf_op jit(solution)/shard_map/ppermute | solution.py:53
  218.2 26.9 %collective-permute-start.48 = (bf16[64,128]{1,0:T(8,128)(2,1)S(1)}, bf16[64,128]{1,0:T(8,128)(2,1)S(1)}, u32[]{:S(2)}, u32[]{:S(2)}) collective-permute-start(bf16[64,128]{1,0:T(8,128)(2,1)S(1)} %get-tuple-element.20), channel_id=1, source_target_pairs={{0,257},{1,258},{2,259},{3,256},{4,261},{5,262},{6,263},{7,260},{8... | collective-permute-start | bytes 49160 | tf_op jit(solution)/shard_map/ppermute | solution.py:53
  (32 other events, 414.8 us)
where the time goes:
time: 272 us; the launch traced here: 271 us
  starting transfers between devices  227 us (83%)
  blocking collectives  16.6 us (6%)
  between operations  7.84 us (3%)
  waiting for transfers between devices  5.56 us (2%)
  matrix products  5.43 us (2%)
  local copies, waits for them, and re-layouts  4.86 us (2%)
  other arithmetic  3.04 us (1%)
    ppermute x48, starting transfers between devices, exchange(): per_shift.append(lax.ppermute(payload, ('area', 'blk'), perm))  205 us
    ppermute x3, starting transfers between devices, body(): provide.append(lax.ppermute(wanted[k], 'area', perm))  17.1 us
    all_gather x1, blocking collectives, body(): post_whole = lax.all_gather(post_sel, 'blk', axis=3, tiled=True)  16.6 us
    ppermute x48, waiting for transfers between devices, exchange(): per_shift.append(lax.ppermute(payload, ('area', 'blk'), perm))  5.55 us
  transfers between devices with their start and end apart: 52, of which 4 were waited for; matrix products, arithmetic and copies ran while one was open for 1% of the time, Pallas kernels for 0%

commit v1 on v0

--- a/solution.py
+++ b/solution.py
@@ -5,6 +5,12 @@
 
 STEPS = 4
 euler_step = 0.5
+
+
+def laid_out(blocks, dim):
+    dims = list(blocks.shape[1:])
+    dims[dim] *= blocks.shape[0]
+    return jnp.moveaxis(blocks, 0, dim).reshape(dims)
 
 
 def centre(x):
@@ -74,7 +80,19 @@
     pre_centered = centre(jnp.stack(pre_list, axis=1))
     post_centered = centre(jnp.stack(post_list, axis=0))
     post_sel = jnp.take(post_centered, slot_dst, axis=1).transpose(1, 0, 2, 3)
-    post_whole = lax.all_gather(post_sel, "blk", axis=3, tiled=True)
+    size = lax.axis_size("blk")
+    pairs = [(i_2, (i_2 + 1) % size) for i_2 in range(size)]
+    back = [(b_2, a) for a, b_2 in pairs]
+    lower, upper = ([], [])
+    for step in range(size - 1):
+        if step % 2 == 0:
+            lower.append(lax.ppermute(lower[-1] if lower else post_sel, "blk", pairs))
+        else:
+            upper.append(lax.ppermute(upper[-1] if upper else post_sel, "blk", back))
+    blocks = jnp.stack([*lower[::-1], post_sel, *upper])
+    shift = lax.axis_index("blk") - len(lower)
+    blocks = blocks[(jnp.arange(size) - shift) % size]
+    post_whole = laid_out(blocks, 3)
     change = jnp.einsum(
         "ktnq,ktnu->kqu", pre_centered, post_whole, preferred_element_type=jnp.float32
     )

time: 272 us -> 275 us (1.011)
  the two profiles are of different devices: /device:TPU:2 before, /device:TPU:1 now
where the time goes in v1:
time: 275 us; the launch traced here: 273 us
  starting transfers between devices  234 us (85%)
  waiting for transfers between devices  16 us (6%)
  between operations  8.26 us (3%)
  local copies, waits for them, and re-layouts  6.19 us (2%)
  matrix products  5.42 us (2%)
  other arithmetic  3.25 us (1%)
    ppermute x48, starting transfers between devices, exchange(): per_shift.append(lax.ppermute(payload, ('area', 'blk'), perm))  203 us
    ppermute x3, starting transfers between devices, body(): provide.append(lax.ppermute(wanted[k], 'area', perm))  17.4 us
    ppermute x48, waiting for transfers between devices, exchange(): per_shift.append(lax.ppermute(payload, ('area', 'blk'), perm))  8.66 us
    ppermute x2, waiting for transfers between devices, body(): lower.append(lax.ppermute(lower[-1] if lower else post_sel, 'blk', pairs))  7.28 us
    ppermute x2, starting transfers between devices, body(): lower.append(lax.ppermute(lower[-1] if lower else post_sel, 'blk', pairs))  7.17 us
  transfers between devices with their start and end apart: 55, of which 10 were waited for; matrix products, arithmetic and copies ran while one was open for 1% of the time, Pallas kernels for 0%

profile of v1, /device:TPU:1, one launch (start us, length us, event | category | flops | bytes accessed | tf_op | source)
XLA Modules:
  0.0 273.0 jit_solution(1511801244197740867)
XLA Ops:
  2.0 8.7 %collective-permute-start = (s32[]{:T(128)}, s32[]{:T(128)}, u32[]{:S(2)}, u32[]{:S(2)}) collective-permute-start(s32[]{:T(128)} %bitcast.2), channel_id=1, source_target_pairs={{0,508},{4,0},{8,4},{12,8},{16,12},{20,16},{24,20},{28,24},{32,28}... | collective-permute-start | bytes 20 | tf_op jit(solution)/shard_map/ppermute | solution.py:39
  10.7 5.3 %collective-permute-start.10 = (s32[]{:T(128)}, s32[]{:T(128)}, u32[]{:S(2)}, u32[]{:S(2)}) collective-permute-start(s32[]{:T(128)} %bitcast.16), channel_id=1, source_target_pairs={{0,256},{4,260},{8,264},{12,268},{16,272},{20,276},{24,280},{28,28... | collective-permute-start | bytes 20 | tf_op jit(solution)/shard_map/ppermute | solution.py:39
  33.8 5.1 %collective-permute-start.4 = (bf16[64,128]{1,0:T(8,128)(2,1)S(1)}, bf16[64,128]{1,0:T(8,128)(2,1)S(1)}, u32[]{:S(2)}, u32[]{:S(2)}) collective-permute-start(bf16[64,128]{1,0:T(8,128)(2,1)S(1)} %get-tuple-element.28), channel_id=1, source_target_pairs={{0,7},{1,4},{2,5},{3,6},{4,11},{5,8},{6,9},{7,10},{8,15},{9,12},{1... | collective-permute-start | bytes 49160 | tf_op jit(solution)/shard_map/ppermute | solution.py:59
  51.6 8.5 %collective-permute-start.13 = (bf16[64,128]{1,0:T(8,128)(2,1)S(1)}, bf16[64,128]{1,0:T(8,128)(2,1)S(1)}, u32[]{:S(2)}, u32[]{:S(2)}) collective-permute-start(bf16[64,128]{1,0:T(8,128)(2,1)S(1)} %get-tuple-element.29), channel_id=1, source_target_pairs={{0,258},{1,259},{2,256},{3,257},{4,262},{5,263},{6,260},{7,261},{8... | collective-permute-start | bytes 49160 | tf_op jit(solution)/shard_map/ppermute | solution.py:59
  62.0 5.8 %collective-permute-start.11 = (bf16[64,128]{1,0:T(8,128)(2,1)S(1)}, bf16[64,128]{1,0:T(8,128)(2,1)S(1)}, u32[]{:S(2)}, u32[]{:S(2)}) collective-permute-start(bf16[64,128]{1,0:T(8,128)(2,1)S(1)} %get-tuple-element.29), channel_id=1, source_target_pairs={{0,256},{1,257},{2,258},{3,259},{4,260},{5,261},{6,262},{7,263},{8... | collective-permute-start | bytes 49160 | tf_op jit(solution)/shard_map/ppermute | solution.py:59
  67.8 6.2 %collective-permute-start.9 = (bf16[64,128]{1,0:T(8,128)(2,1)S(1)}, bf16[64,128]{1,0:T(8,128)(2,1)S(1)}, u32[]{:S(2)}, u32[]{:S(2)}) collective-permute-start(bf16[64,128]{1,0:T(8,128)(2,1)S(1)} %get-tuple-element.30), channel_id=1, source_target_pairs={{0,511},{1,508},{2,509},{3,510},{4,3},{5,0},{6,1},{7,2},{8,7},{9,4... | collective-permute-start | bytes 49160 | tf_op jit(solution)/shard_map/ppermute | solution.py:59
  74.1 5.5 %collective-permute-start.8 = (bf16[64,128]{1,0:T(8,128)(2,1)S(1)}, bf16[64,128]{1,0:T(8,128)(2,1)S(1)}, u32[]{:S(2)}, u32[]{:S(2)}) collective-permute-start(bf16[64,128]{1,0:T(8,128)(2,1)S(1)} %get-tuple-element.30), channel_id=1, source_target_pairs={{0,510},{1,511},{2,508},{3,509},{4,2},{5,3},{6,0},{7,1},{8,6},{9,7... | collective-permute-start | bytes 49160 | tf_op jit(solution)/shard_map/ppermute | solution.py:59
  89.2 4.6 %collective-permute-start.18 = (bf16[64,128]{1,0:T(8,128)(2,1)S(1)}, bf16[64,128]{1,0:T(8,128)(2,1)S(1)}, u32[]{:S(2)}, u32[]{:S(2)}) collective-permute-start(bf16[64,128]{1,0:T(8,128)(2,1)S(1)} %get-tuple-element.25), channel_id=1, source_target_pairs={{0,7},{1,4},{2,5},{3,6},{4,11},{5,8},{6,9},{7,10},{8,15},{9,12},{1... | collective-permute-start | bytes 49160 | tf_op jit(solution)/shard_map/ppermute | solution.py:59
  100.3 7.2 %collective-permute-start.26 = (bf16[64,128]{1,0:T(8,128)(2,1)S(1)}, bf16[64,128]{1,0:T(8,128)(2,1)S(1)}, u32[]{:S(2)}, u32[]{:S(2)}) collective-permute-start(bf16[64,128]{1,0:T(8,128)(2,1)S(1)} %get-tuple-element.26), channel_id=1, source_target_pairs={{0,259},{1,256},{2,257},{3,258},{4,263},{5,260},{6,261},{7,262},{8... | collective-permute-start | bytes 49160 | tf_op jit(solution)/shard_map/ppermute | solution.py:59
  107.6 5.0 %collective-permute-start.25 = (bf16[64,128]{1,0:T(8,128)(2,1)S(1)}, bf16[64,128]{1,0:T(8,128)(2,1)S(1)}, u32[]{:S(2)}, u32[]{:S(2)}) collective-permute-start(bf16[64,128]{1,0:T(8,128)(2,1)S(1)} %get-tuple-element.26), channel_id=1, source_target_pairs={{0,258},{1,259},{2,256},{3,257},{4,262},{5,263},{6,260},{7,261},{8... | collective-permute-start | bytes 49160 | tf_op jit(solution)/shard_map/ppermute | solution.py:59
  112.6 5.1 %collective-permute-start.24 = (bf16[64,128]{1,0:T(8,128)(2,1)S(1)}, bf16[64,128]{1,0:T(8,128)(2,1)S(1)}, u32[]{:S(2)}, u32[]{:S(2)}) collective-permute-start(bf16[64,128]{1,0:T(8,128)(2,1)S(1)} %get-tuple-element.26), channel_id=1, source_target_pairs={{0,257},{1,258},{2,259},{3,256},{4,261},{5,262},{6,263},{7,260},{8... | collective-permute-start | bytes 49160 | tf_op jit(solution)/shard_map/ppermute | solution.py:59
  120.8 5.8 %collective-permute-start.22 = (bf16[64,128]{1,0:T(8,128)(2,1)S(1)}, bf16[64,128]{1,0:T(8,128)(2,1)S(1)}, u32[]{:S(2)}, u32[]{:S(2)}) collective-permute-start(bf16[64,128]{1,0:T(8,128)(2,1)S(1)} %get-tuple-element.27), channel_id=1, source_target_pairs={{0,511},{1,508},{2,509},{3,510},{4,3},{5,0},{6,1},{7,2},{8,7},{9,4... | collective-permute-start | bytes 49160 | tf_op jit(solution)/shard_map/ppermute | solution.py:59
  126.6 7.1 %collective-permute-start.21 = (bf16[64,128]{1,0:T(8,128)(2,1)S(1)}, bf16[64,128]{1,0:T(8,128)(2,1)S(1)}, u32[]{:S(2)}, u32[]{:S(2)}) collective-permute-start(bf16[64,128]{1,0:T(8,128)(2,1)S(1)} %get-tuple-element.27), channel_id=1, source_target_pairs={{0,510},{1,511},{2,508},{3,509},{4,2},{5,3},{6,0},{7,1},{8,6},{9,7... | collective-permute-start | bytes 49160 | tf_op jit(solution)/shard_map/ppermute | solution.py:59
  143.2 4.7 %collective-permute-start.30 = (bf16[64,128]{1,0:T(8,128)(2,1)S(1)}, bf16[64,128]{1,0:T(8,128)(2,1)S(1)}, u32[]{:S(2)}, u32[]{:S(2)}) collective-permute-start(bf16[64,128]{1,0:T(8,128)(2,1)S(1)} %get-tuple-element.22), channel_id=1, source_target_pairs={{0,7},{1,4},{2,5},{3,6},{4,11},{5,8},{6,9},{7,10},{8,15},{9,12},{1... | collective-permute-start | bytes 49160 | tf_op jit(solution)/shard_map/ppermute | solution.py:59
  153.8 9.0 %collective-permute-start.38 = (bf16[64,128]{1,0:T(8,128)(2,1)S(1)}, bf16[64,128]{1,0:T(8,128)(2,1)S(1)}, u32[]{:S(2)}, u32[]{:S(2)}) collective-permute-start(bf16[64,128]{1,0:T(8,128)(2,1)S(1)} %get-tuple-element.23), channel_id=1, source_target_pairs={{0,259},{1,256},{2,257},{3,258},{4,263},{5,260},{6,261},{7,262},{8... | collective-permute-start | bytes 49160 | tf_op jit(solution)/shard_map/ppermute | solution.py:59
  165.7 6.0 %collective-permute-start.36 = (bf16[64,128]{1,0:T(8,128)(2,1)S(1)}, bf16[64,128]{1,0:T(8,128)(2,1)S(1)}, u32[]{:S(2)}, u32[]{:S(2)}) collective-permute-start(bf16[64,128]{1,0:T(8,128)(2,1)S(1)} %get-tuple-element.23), channel_id=1, source_target_pairs={{0,257},{1,258},{2,259},{3,256},{4,261},{5,262},{6,263},{7,260},{8... | collective-permute-start | bytes 49160 | tf_op jit(solution)/shard_map/ppermute | solution.py:59
  174.2 6.3 %collective-permute-start.34 = (bf16[64,128]{1,0:T(8,128)(2,1)S(1)}, bf16[64,128]{1,0:T(8,128)(2,1)S(1)}, u32[]{:S(2)}, u32[]{:S(2)}) collective-permute-start(bf16[64,128]{1,0:T(8,128)(2,1)S(1)} %get-tuple-element.24), channel_id=1, source_target_pairs={{0,511},{1,508},{2,509},{3,510},{4,3},{5,0},{6,1},{7,2},{8,7},{9,4... | collective-permute-start | bytes 49160 | tf_op jit(solution)/shard_map/ppermute | solution.py:59
  180.6 7.9 %collective-permute-start.33 = (bf16[64,128]{1,0:T(8,128)(2,1)S(1)}, bf16[64,128]{1,0:T(8,128)(2,1)S(1)}, u32[]{:S(2)}, u32[]{:S(2)}) collective-permute-start(bf16[64,128]{1,0:T(8,128)(2,1)S(1)} %get-tuple-element.24), channel_id=1, source_target_pairs={{0,510},{1,511},{2,508},{3,509},{4,2},{5,3},{6,0},{7,1},{8,6},{9,7... | collective-permute-start | bytes 49160 | tf_op jit(solution)/shard_map/ppermute | solution.py:59
  197.9 4.6 %collective-permute-start.42 = (bf16[64,128]{1,0:T(8,128)(2,1)S(1)}, bf16[64,128]{1,0:T(8,128)(2,1)S(1)}, u32[]{:S(2)}, u32[]{:S(2)}) collective-permute-start(bf16[64,128]{1,0:T(8,128)(2,1)S(1)} %get-tuple-element.19), channel_id=1, source_target_pairs={{0,7},{1,4},{2,5},{3,6},{4,11},{5,8},{6,9},{7,10},{8,15},{9,12},{1... | collective-permute-start | bytes 49160 | tf_op jit(solution)/shard_map/ppermute | solution.py:59
  208.5 8.0 %collective-permute-start.50 = (bf16[64,128]{1,0:T(8,128)(2,1)S(1)}, bf16[64,128]{1,0:T(8,128)(2,1)S(1)}, u32[]{:S(2)}, u32[]{:S(2)}) collective-permute-start(bf16[64,128]{1,0:T(8,128)(2,1)S(1)} %get-tuple-element.20), channel_id=1, source_target_pairs={{0,259},{1,256},{2,257},{3,258},{4,263},{5,260},{6,261},{7,262},{8... | collective-permute-start | bytes 49160 | tf_op jit(solution)/shard_map/ppermute | solution.py:59
  219.5 6.9 %collective-permute-start.48 = (bf16[64,128]{1,0:T(8,128)(2,1)S(1)}, bf16[64,128]{1,0:T(8,128)(2,1)S(1)}, u32[]{:S(2)}, u32[]{:S(2)}) collective-permute-start(bf16[64,128]{1,0:T(8,128)(2,1)S(1)} %get-tuple-element.20), channel_id=1, source_target_pairs={{0,257},{1,258},{2,259},{3,256},{4,261},{5,262},{6,263},{7,260},{8... | collective-permute-start | bytes 49160 | tf_op jit(solution)/shard_map/ppermute | solution.py:59
  229.0 6.3 %collective-permute-start.46 = (bf16[64,128]{1,0:T(8,128)(2,1)S(1)}, bf16[64,128]{1,0:T(8,128)(2,1)S(1)}, u32[]{:S(2)}, u32[]{:S(2)}) collective-permute-start(bf16[64,128]{1,0:T(8,128)(2,1)S(1)} %get-tuple-element.21), channel_id=1, source_target_pairs={{0,511},{1,508},{2,509},{3,510},{4,3},{5,0},{6,1},{7,2},{8,7},{9,4... | collective-permute-start | bytes 49160 | tf_op jit(solution)/shard_map/ppermute | solution.py:59
  235.3 7.1 %collective-permute-start.45 = (bf16[64,128]{1,0:T(8,128)(2,1)S(1)}, bf16[64,128]{1,0:T(8,128)(2,1)S(1)}, u32[]{:S(2)}, u32[]{:S(2)}) collective-permute-start(bf16[64,128]{1,0:T(8,128)(2,1)S(1)} %get-tuple-element.21), channel_id=1, source_target_pairs={{0,510},{1,511},{2,508},{3,509},{4,2},{5,3},{6,0},{7,1},{8,6},{9,7... | collective-permute-start | bytes 49160 | tf_op jit(solution)/shard_map/ppermute | solution.py:59
  266.1 5.1 %collective-permute-done.52 = bf16[3,4,64,128]{3,2,1,0:T(8,128)(2,1)S(1)} collective-permute-done((bf16[3,4,64,128]{3,2,1,0:T(8,128)(2,1)S(1)}, bf16[3,4,64,128]{3,2,1,0:T(8,128)(2,1)S(1)}, u32[]{:S(2)}, u32[]{:S(2)}) %collective-permute-start.52) | collective-permute-done | bytes 196640 | tf_op jit(solution)/shard_map/ppermute | solution.py:89
  (152 shorter events, 112.8 us)
Async XLA Ops:
  2.0 25.9 %collective-permute-start = (s32[]{:T(128)}, s32[]{:T(128)}, u32[]{:S(2)}, u32[]{:S(2)}) collective-permute-start(s32[]{:T(128)} %bitcast.2), channel_id=1, source_target_pairs={{0,508},{4,0},{8,4},{12,8},{16,12},{20,16},{24,20},{28,24},{32,28}... | collective-permute-start | bytes 20 | tf_op jit(solution)/shard_map/ppermute | solution.py:39
  21.5 65.7 %all-to-all-start = ((bf16[3,128,4,128]{3,1,0,2:T(8,128)(2,1)}), bf16[3,128,4,128]{3,1,0,2:T(8,128)(2,1)S(1)}, u32[]{:S(2)}, u32[]{:S(2)}) async-start(bf16[3,128,4,128]{3,1,0,2:T(8,128)(2,1)} %copy.74), calls=%async_computation | async-start | bytes 786432 | tf_op jit(solution)/shard_map/all_to_all | solution.py:41
  45.1 22.7 %collective-permute-start.1 = (bf16[64,128]{1,0:T(8,128)(2,1)S(1)}, bf16[64,128]{1,0:T(8,128)(2,1)S(1)}, u32[]{:S(2)}, u32[]{:S(2)}) collective-permute-start(bf16[64,128]{1,0:T(8,128)(2,1)S(1)} %get-tuple-element.28), channel_id=1, source_target_pairs={{0,4},{1,5},{2,6},{3,7},{4,8},{5,9},{6,10},{7,11},{8,12},{9,13},{1... | collective-permute-start | bytes 49160 | tf_op jit(solution)/shard_map/ppermute | solution.py:59
  48.1 25.9 %collective-permute-start.14 = (bf16[64,128]{1,0:T(8,128)(2,1)S(1)}, bf16[64,128]{1,0:T(8,128)(2,1)S(1)}, u32[]{:S(2)}, u32[]{:S(2)}) collective-permute-start(bf16[64,128]{1,0:T(8,128)(2,1)S(1)} %get-tuple-element.29), channel_id=1, source_target_pairs={{0,259},{1,256},{2,257},{3,258},{4,263},{5,260},{6,261},{7,262},{8... | collective-permute-start | bytes 49160 | tf_op jit(solution)/shard_map/ppermute | solution.py:59
  51.6 28.0 %collective-permute-start.13 = (bf16[64,128]{1,0:T(8,128)(2,1)S(1)}, bf16[64,128]{1,0:T(8,128)(2,1)S(1)}, u32[]{:S(2)}, u32[]{:S(2)}) collective-permute-start(bf16[64,128]{1,0:T(8,128)(2,1)S(1)} %get-tuple-element.29), channel_id=1, source_target_pairs={{0,258},{1,259},{2,256},{3,257},{4,262},{5,263},{6,260},{7,261},{8... | collective-permute-start | bytes 49160 | tf_op jit(solution)/shard_map/ppermute | solution.py:59
  60.1 22.1 %collective-permute-start.12 = (bf16[64,128]{1,0:T(8,128)(2,1)S(1)}, bf16[64,128]{1,0:T(8,128)(2,1)S(1)}, u32[]{:S(2)}, u32[]{:S(2)}) collective-permute-start(bf16[64,128]{1,0:T(8,128)(2,1)S(1)} %get-tuple-element.29), channel_id=1, source_target_pairs={{0,257},{1,258},{2,259},{3,256},{4,261},{5,262},{6,263},{7,260},{8... | collective-permute-start | bytes 49160 | tf_op jit(solution)/shard_map/ppermute | solution.py:59
  62.0 22.8 %collective-permute-start.11 = (bf16[64,128]{1,0:T(8,128)(2,1)S(1)}, bf16[64,128]{1,0:T(8,128)(2,1)S(1)}, u32[]{:S(2)}, u32[]{:S(2)}) collective-permute-start(bf16[64,128]{1,0:T(8,128)(2,1)S(1)} %get-tuple-element.29), channel_id=1, source_target_pairs={{0,256},{1,257},{2,258},{3,259},{4,260},{5,261},{6,262},{7,263},{8... | collective-permute-start | bytes 49160 | tf_op jit(solution)/shard_map/ppermute | solution.py:59
  95.8 21.9 %collective-permute-start.16 = (bf16[64,128]{1,0:T(8,128)(2,1)S(1)}, bf16[64,128]{1,0:T(8,128)(2,1)S(1)}, u32[]{:S(2)}, u32[]{:S(2)}) collective-permute-start(bf16[64,128]{1,0:T(8,128)(2,1)S(1)} %get-tuple-element.25), channel_id=1, source_target_pairs={{0,5},{1,6},{2,7},{3,4},{4,9},{5,10},{6,11},{7,8},{8,13},{9,14},{1... | collective-permute-start | bytes 49160 | tf_op jit(solution)/shard_map/ppermute | solution.py:59
  97.8 23.0 %collective-permute-start.15 = (bf16[64,128]{1,0:T(8,128)(2,1)S(1)}, bf16[64,128]{1,0:T(8,128)(2,1)S(1)}, u32[]{:S(2)}, u32[]{:S(2)}) collective-permute-start(bf16[64,128]{1,0:T(8,128)(2,1)S(1)} %get-tuple-element.25), channel_id=1, source_target_pairs={{0,4},{1,5},{2,6},{3,7},{4,8},{5,9},{6,10},{7,11},{8,12},{9,13},{1... | collective-permute-start | bytes 49160 | tf_op jit(solution)/shard_map/ppermute | solution.py:59
  100.3 26.2 %collective-permute-start.26 = (bf16[64,128]{1,0:T(8,128)(2,1)S(1)}, bf16[64,128]{1,0:T(8,128)(2,1)S(1)}, u32[]{:S(2)}, u32[]{:S(2)}) collective-permute-start(bf16[64,128]{1,0:T(8,128)(2,1)S(1)} %get-tuple-element.26), channel_id=1, source_target_pairs={{0,259},{1,256},{2,257},{3,258},{4,263},{5,260},{6,261},{7,262},{8... | collective-permute-start | bytes 49160 | tf_op jit(solution)/shard_map/ppermute | solution.py:59
  107.6 26.2 %collective-permute-start.25 = (bf16[64,128]{1,0:T(8,128)(2,1)S(1)}, bf16[64,128]{1,0:T(8,128)(2,1)S(1)}, u32[]{:S(2)}, u32[]{:S(2)}) collective-permute-start(bf16[64,128]{1,0:T(8,128)(2,1)S(1)} %get-tuple-element.26), channel_id=1, source_target_pairs={{0,258},{1,259},{2,256},{3,257},{4,262},{5,263},{6,260},{7,261},{8... | collective-permute-start | bytes 49160 | tf_op jit(solution)/shard_map/ppermute | solution.py:59
  112.6 24.3 %collective-permute-start.24 = (bf16[64,128]{1,0:T(8,128)(2,1)S(1)}, bf16[64,128]{1,0:T(8,128)(2,1)S(1)}, u32[]{:S(2)}, u32[]{:S(2)}) collective-permute-start(bf16[64,128]{1,0:T(8,128)(2,1)S(1)} %get-tuple-element.26), channel_id=1, source_target_pairs={{0,257},{1,258},{2,259},{3,256},{4,261},{5,262},{6,263},{7,260},{8... | collective-permute-start | bytes 49160 | tf_op jit(solution)/shard_map/ppermute | solution.py:59
  117.7 22.3 %collective-permute-start.23 = (bf16[64,128]{1,0:T(8,128)(2,1)S(1)}, bf16[64,128]{1,0:T(8,128)(2,1)S(1)}, u32[]{:S(2)}, u32[]{:S(2)}) collective-permute-start(bf16[64,128]{1,0:T(8,128)(2,1)S(1)} %get-tuple-element.26), channel_id=1, source_target_pairs={{0,256},{1,257},{2,258},{3,259},{4,260},{5,261},{6,262},{7,263},{8... | collective-permute-start | bytes 49160 | tf_op jit(solution)/shard_map/ppermute | solution.py:59
  151.9 22.4 %collective-permute-start.27 = (bf16[64,128]{1,0:T(8,128)(2,1)S(1)}, bf16[64,128]{1,0:T(8,128)(2,1)S(1)}, u32[]{:S(2)}, u32[]{:S(2)}) collective-permute-start(bf16[64,128]{1,0:T(8,128)(2,1)S(1)} %get-tuple-element.22), channel_id=1, source_target_pairs={{0,4},{1,5},{2,6},{3,7},{4,8},{5,9},{6,10},{7,11},{8,12},{9,13},{1... | collective-permute-start | bytes 49160 | tf_op jit(solution)/shard_map/ppermute | solution.py:59
  153.8 26.8 %collective-permute-start.38 = (bf16[64,128]{1,0:T(8,128)(2,1)S(1)}, bf16[64,128]{1,0:T(8,128)(2,1)S(1)}, u32[]{:S(2)}, u32[]{:S(2)}) collective-permute-start(bf16[64,128]{1,0:T(8,128)(2,1)S(1)} %get-tuple-element.23), channel_id=1, source_target_pairs={{0,259},{1,256},{2,257},{3,258},{4,263},{5,260},{6,261},{7,262},{8... | collective-permute-start | bytes 49160 | tf_op jit(solution)/shard_map/ppermute | solution.py:59
  162.8 25.7 %collective-permute-start.37 = (bf16[64,128]{1,0:T(8,128)(2,1)S(1)}, bf16[64,128]{1,0:T(8,128)(2,1)S(1)}, u32[]{:S(2)}, u32[]{:S(2)}) collective-permute-start(bf16[64,128]{1,0:T(8,128)(2,1)S(1)} %get-tuple-element.23), channel_id=1, source_target_pairs={{0,258},{1,259},{2,256},{3,257},{4,262},{5,263},{6,260},{7,261},{8... | collective-permute-start | bytes 49160 | tf_op jit(solution)/shard_map/ppermute | solution.py:59
  165.7 25.8 %collective-permute-start.36 = (bf16[64,128]{1,0:T(8,128)(2,1)S(1)}, bf16[64,128]{1,0:T(8,128)(2,1)S(1)}, u32[]{:S(2)}, u32[]{:S(2)}) collective-permute-start(bf16[64,128]{1,0:T(8,128)(2,1)S(1)} %get-tuple-element.23), channel_id=1, source_target_pairs={{0,257},{1,258},{2,259},{3,256},{4,261},{5,262},{6,263},{7,260},{8... | collective-permute-start | bytes 49160 | tf_op jit(solution)/shard_map/ppermute | solution.py:59
  171.7 22.4 %collective-permute-start.35 = (bf16[64,128]{1,0:T(8,128)(2,1)S(1)}, bf16[64,128]{1,0:T(8,128)(2,1)S(1)}, u32[]{:S(2)}, u32[]{:S(2)}) collective-permute-start(bf16[64,128]{1,0:T(8,128)(2,1)S(1)} %get-tuple-element.23), channel_id=1, source_target_pairs={{0,256},{1,257},{2,258},{3,259},{4,260},{5,261},{6,262},{7,263},{8... | collective-permute-start | bytes 49160 | tf_op jit(solution)/shard_map/ppermute | solution.py:59
  204.5 22.0 %collective-permute-start.40 = (bf16[64,128]{1,0:T(8,128)(2,1)S(1)}, bf16[64,128]{1,0:T(8,128)(2,1)S(1)}, u32[]{:S(2)}, u32[]{:S(2)}) collective-permute-start(bf16[64,128]{1,0:T(8,128)(2,1)S(1)} %get-tuple-element.19), channel_id=1, source_target_pairs={{0,5},{1,6},{2,7},{3,4},{4,9},{5,10},{6,11},{7,8},{8,13},{9,14},{1... | collective-permute-start | bytes 49160 | tf_op jit(solution)/shard_map/ppermute | solution.py:59
  206.4 22.6 %collective-permute-start.39 = (bf16[64,128]{1,0:T(8,128)(2,1)S(1)}, bf16[64,128]{1,0:T(8,128)(2,1)S(1)}, u32[]{:S(2)}, u32[]{:S(2)}) collective-permute-start(bf16[64,128]{1,0:T(8,128)(2,1)S(1)} %get-tuple-element.19), channel_id=1, source_target_pairs={{0,4},{1,5},{2,6},{3,7},{4,8},{5,9},{6,10},{7,11},{8,12},{9,13},{1... | collective-permute-start | bytes 49160 | tf_op jit(solution)/shard_map/ppermute | solution.py:59
  208.5 26.9 %collective-permute-start.50 = (bf16[64,128]{1,0:T(8,128)(2,1)S(1)}, bf16[64,128]{1,0:T(8,128)(2,1)S(1)}, u32[]{:S(2)}, u32[]{:S(2)}) collective-permute-start(bf16[64,128]{1,0:T(8,128)(2,1)S(1)} %get-tuple-element.20), channel_id=1, source_target_pairs={{0,259},{1,256},{2,257},{3,258},{4,263},{5,260},{6,261},{7,262},{8... | collective-permute-start | bytes 49160 | tf_op jit(solution)/shard_map/ppermute | solution.py:59
  216.5 26.0 %collective-permute-start.49 = (bf16[64,128]{1,0:T(8,128)(2,1)S(1)}, bf16[64,128]{1,0:T(8,128)(2,1)S(1)}, u32[]{:S(2)}, u32[]{:S(2)}) collective-permute-start(bf16[64,128]{1,0:T(8,128)(2,1)S(1)} %get-tuple-element.20), channel_id=1, source_target_pairs={{0,258},{1,259},{2,256},{3,257},{4,262},{5,263},{6,260},{7,261},{8... | collective-permute-start | bytes 49160 | tf_op jit(solution)/shard_map/ppermute | solution.py:59
  219.5 26.2 %collective-permute-start.48 = (bf16[64,128]{1,0:T(8,128)(2,1)S(1)}, bf16[64,128]{1,0:T(8,128)(2,1)S(1)}, u32[]{:S(2)}, u32[]{:S(2)}) collective-permute-start(bf16[64,128]{1,0:T(8,128)(2,1)S(1)} %get-tuple-element.20), channel_id=1, source_target_pairs={{0,257},{1,258},{2,259},{3,256},{4,261},{5,262},{6,263},{7,260},{8... | collective-permute-start | bytes 49160 | tf_op jit(solution)/shard_map/ppermute | solution.py:59
  226.5 22.3 %collective-permute-start.47 = (bf16[64,128]{1,0:T(8,128)(2,1)S(1)}, bf16[64,128]{1,0:T(8,128)(2,1)S(1)}, u32[]{:S(2)}, u32[]{:S(2)}) collective-permute-start(bf16[64,128]{1,0:T(8,128)(2,1)S(1)} %get-tuple-element.20), channel_id=1, source_target_pairs={{0,256},{1,257},{2,258},{3,259},{4,260},{5,261},{6,262},{7,263},{8... | collective-permute-start | bytes 49160 | tf_op jit(solution)/shard_map/ppermute | solution.py:59
  (35 other events, 432.5 us)
